TPU v7x, 256 devices: a whole 4x4x8 slice. The times are simulated.
256 devices in a mesh: cfg: 2 (over core), req: 8 (over z), seq: 16 (over y, x).
Axes of the slice: x: 4, y: 4, z: 8, core: 2. Of those that a mesh axis runs over, the one named last changes fastest.
Arguments:
- img_hidden: bfloat16 [2, 16, 512, 1536], P('cfg', 'req', 'seq'), may hold values from -6 to 6
- txt_hidden: bfloat16 [2, 16, 160, 1536], P('cfg', 'req', 'seq'), may hold values from -6 to 6
- text_len: int32 [2, 16], P('cfg'), may hold values from 1 to 154, as said below
- pooled: float32 [2, 16, 1536], P('cfg'), may hold values from -6 to 6
- timestep: int32 [16], replicated, may hold values from 0 to 27
- latent: float32 [16, 512, 64], P('req', 'seq', 'cfg'), may hold values from -24 to 24
- mod_weight: bfloat16 [1536, 15360], P(None, ('req', 'seq')), may hold values from -0.15625 to 0.15625
- mod_bias: float32 [15360], P(('req', 'seq')), may hold values from -2 to 2
- img_qkv: bfloat16 [1536, 3, 1536], P(None, None, 'req'), may hold values from -2.5 to 2.5
- txt_kv: bfloat16 [1536, 2, 1536], P(None, None, 'req'), may hold values from -0.15625 to 0.15625
- out_weight: bfloat16 [1536, 1536], P('req'), may hold values from -0.15625 to 0.15625
- fc_in: bfloat16 [1536, 6144], P(None, 'seq'), may hold values from -0.15625 to 0.15625
- fc_out: bfloat16 [6144, 1536], P('seq'), may hold values from -0.078125 to 0.078125
- final_weight: bfloat16 [1536, 64], replicated, may hold values from -0.15625 to 0.15625
Outputs:
- velocity: float32 [16, 512, 64], P('req', 'seq', 'cfg')
- next_latent: float32 [16, 512, 64], P('req', 'seq', 'cfg')
- latent_norm: float32 [16], P('req')
- latent_peak: float32 [16], P('req')
Inputs may be any that keep to these rules, and one draw needn't show every extreme that they name: Text slots from text_len to 159 of a request are padding; every draw has a request of length 154 and one of length 1.
All inputs are finite; a program needn't handle non-finite values.
Results may differ from a plain program's by a relative error of at most 0.015.
Values may be sent and summed in bfloat16 or wider, within the bound.
No kernel may reach another device: no remote copies, remote signals or barrier semaphores. Data moves between devices by JAX's collectives and lax.ppermute only.
A program may use at most 64 MiB of HBM per device.

v0:
```python
import math
import jax
import jax.numpy as jnp
from jax import lax
from jax.sharding import PartitionSpec as P

D = 1536
HD = 64
PATCHC = 64
IMG = 512
STEPS = 28
SIGMA_SHIFT = 3.0
GUIDANCE = 5.0
EPSILON = 1e-06
MASKED_SCORE = -1e30


def from_partner(value, axis, distance):
    mask = 2**distance
    pairs = [(source, source ^ mask) for source in range(lax.axis_size(axis))]
    return lax.ppermute(value, axis, pairs)


def shifted(fraction):
    return SIGMA_SHIFT * fraction / (1.0 + (SIGMA_SHIFT - 1.0) * fraction)


def plan(timestep):
    position = timestep.astype(jnp.float32)
    return (shifted(1.0 - position / STEPS), shifted(1.0 - (position + 1.0) / STEPS))


def time_features(sigma):
    half_width = D // 2
    frequency = jnp.exp(-math.log(10000.0) * jnp.arange(half_width, dtype=jnp.float32) / half_width)
    angles = (1000.0 * sigma)[:, None] * frequency[None, :]
    return jnp.concatenate([jnp.cos(angles), jnp.sin(angles)], axis=1)


def layer_norm(values):
    average = jnp.mean(values, axis=-1, keepdims=True)
    centred = values - average
    spread = jnp.mean(centred * centred, axis=-1, keepdims=True)
    return centred * lax.rsqrt(spread + EPSILON)


def attention(queries, key_rows, value_rows, live_keys):
    query_count = queries.shape[0]
    head_count = queries.shape[1]
    block_rows = min(512, query_count)
    scale_factor = HD ** (-0.5)

    def one_block(query_block):
        scores = (
            jnp.einsum("qhd,khd->hqk", query_block, key_rows, preferred_element_type=jnp.float32)
            * scale_factor
        )
        scores = jnp.where(live_keys[None, None, :], scores, MASKED_SCORE)
        highest = jnp.max(scores, axis=-1, keepdims=True)
        exp_scores = jnp.exp(scores - highest)
        weights = (exp_scores / jnp.sum(exp_scores, axis=-1, keepdims=True)).astype(jnp.bfloat16)
        mixture = jnp.einsum(
            "hqk,khd->qhd", weights, value_rows, preferred_element_type=jnp.float32
        )
        return mixture.astype(jnp.bfloat16)

    blocks = queries.reshape(query_count // block_rows, block_rows, head_count, HD)
    return lax.map(one_block, blocks).reshape(query_count, head_count * HD)


def on_device(
    img_hidden,
    txt_hidden,
    text_len,
    pooled,
    timestep,
    latent,
    mod_weight,
    mod_bias,
    img_qkv,
    txt_kv,
    out_weight,
    fc_in,
    fc_out,
    final_weight,
):
    group_size = img_hidden.shape[1]
    current, upcoming = plan(timestep)
    activated = jax.nn.silu(pooled[0] + time_features(current)).astype(jnp.bfloat16)
    columns = jnp.dot(activated, mod_weight, preferred_element_type=jnp.float32) + mod_bias
    every_mod = lax.all_gather(columns, ("req", "seq"), axis=1, tiled=True)
    offset = lax.axis_index("req") * group_size
    modulation = lax.dynamic_slice_in_dim(every_mod, offset, group_size, 0).reshape(
        group_size, 10, 1, D
    )
    shift_attn, scale_attn, gate_attn = (modulation[:, 0], modulation[:, 1], modulation[:, 2])
    shift_mlp, scale_mlp, gate_mlp = (modulation[:, 3], modulation[:, 4], modulation[:, 5])
    shift_text, scale_text = (modulation[:, 6], modulation[:, 7])
    scale_final, shift_final = (modulation[:, 8], modulation[:, 9])
    img_float = img_hidden[0].astype(jnp.float32)
    img_in = (layer_norm(img_float) * (1.0 + scale_attn) + shift_attn).astype(jnp.bfloat16)
    txt_in = (
        layer_norm(txt_hidden[0].astype(jnp.float32)) * (1.0 + scale_text) + shift_text
    ).astype(jnp.bfloat16)
    all_img, all_txt = (
        lax.all_gather(img_in, "req", axis=0, tiled=True),
        lax.all_gather(txt_in, "req", axis=0, tiled=True),
    )
    head_width = img_qkv.shape[2]
    local_heads = head_width // HD
    qkv_columns = img_qkv.reshape(D, 3 * head_width)
    kv_columns = txt_kv.reshape(D, 2 * head_width)
    own_img, own_txt = (
        lax.all_to_all(all_img, "seq", split_axis=0, concat_axis=1, tiled=True),
        lax.all_to_all(all_txt, "seq", split_axis=0, concat_axis=1, tiled=True),
    )
    own_proj = jnp.einsum(
        "rnd,dc->rnc", own_img, qkv_columns, preferred_element_type=jnp.float32
    ).astype(jnp.bfloat16)
    own_proj_txt = jnp.einsum(
        "rnd,dc->rnc", own_txt, kv_columns, preferred_element_type=jnp.float32
    ).astype(jnp.bfloat16)
    local_count = own_proj.shape[0]
    image_rows = own_proj.shape[1]
    text_rows = own_proj_txt.shape[1]
    first_request = lax.axis_index("seq") * local_count

    def attend_request(operands):
        projected, projected_txt, request_slot = operands
        queries = projected[:, :head_width]
        key_rows = jnp.concatenate(
            [projected[:, head_width : 2 * head_width], projected_txt[:, :head_width]], axis=0
        )
        value_rows = jnp.concatenate(
            [projected[:, 2 * head_width :], projected_txt[:, head_width:]], axis=0
        )
        text_count = lax.dynamic_index_in_dim(text_len[0], first_request + request_slot, 0, False)
        live_keys = jnp.arange(image_rows + text_rows, dtype=jnp.int32) < image_rows + text_count
        total_keys = image_rows + text_rows
        return attention(
            queries.reshape(image_rows, local_heads, HD),
            key_rows.reshape(total_keys, local_heads, HD),
            value_rows.reshape(total_keys, local_heads, HD),
            live_keys,
        )

    attended = lax.map(
        attend_request, (own_proj, own_proj_txt, jnp.arange(local_count, dtype=jnp.int32))
    )
    projected_rows = jnp.einsum(
        "rnk,kd->rnd", attended, out_weight, preferred_element_type=jnp.float32
    )
    moved_rows = lax.all_to_all(
        projected_rows.astype(jnp.bfloat16), "seq", split_axis=1, concat_axis=0, tiled=True
    ).astype(projected_rows.dtype)
    attn_out = lax.psum_scatter(
        moved_rows.astype(jnp.bfloat16), "req", scatter_dimension=0, tiled=True
    ).astype(jnp.float32)
    img_mid = img_float + gate_attn * attn_out
    mlp_in = (layer_norm(img_mid) * (1.0 + scale_mlp) + shift_mlp).astype(jnp.bfloat16)
    raised = jnp.einsum(
        "rnd,df->rnf",
        lax.all_gather(mlp_in, "seq", axis=1, tiled=True),
        fc_in,
        preferred_element_type=jnp.float32,
    )
    hidden = jax.nn.gelu(raised, approximate=True).astype(jnp.bfloat16)
    mlp_terms = jnp.einsum("rnf,fd->rnd", hidden, fc_out, preferred_element_type=jnp.float32)
    mlp_out = lax.psum_scatter(
        mlp_terms.astype(jnp.bfloat16), "seq", scatter_dimension=1, tiled=True
    ).astype(jnp.float32)
    img_out = img_mid + gate_mlp * mlp_out
    final_in = (layer_norm(img_out) * (1.0 + scale_final) + shift_final).astype(jnp.bfloat16)
    own_velocity = jnp.einsum(
        "rnd,dc->rnc", final_in, final_weight, preferred_element_type=jnp.float32
    )
    half_values = latent.shape[2]
    half_index = lax.axis_index("cfg")
    kept_velocity = lax.dynamic_slice_in_dim(own_velocity, half_index * half_values, half_values, 2)
    sent_velocity = lax.dynamic_slice_in_dim(
        own_velocity, (1 - half_index) * half_values, half_values, 2
    )
    other_velocity = from_partner(sent_velocity, "cfg", 0)
    cond_first = half_index == 0
    conditional = jnp.where(cond_first, kept_velocity, other_velocity)
    unconditional = jnp.where(cond_first, other_velocity, kept_velocity)
    guided = unconditional + GUIDANCE * (conditional - unconditional)
    step_size = lax.dynamic_slice_in_dim(upcoming - current, offset, group_size, 0)
    next_latent = latent + step_size[:, None, None] * guided
    squares = jnp.sum(next_latent * next_latent, axis=(1, 2))
    largest = jnp.max(jnp.abs(next_latent), axis=(1, 2))
    square_total = lax.psum(squares, ("cfg", "seq"))
    peak_value = lax.pmax(largest, ("cfg", "seq"))
    latent_norm = jnp.sqrt(square_total / (IMG * PATCHC))
    return (guided, next_latent, latent_norm, peak_value)


def solution(mesh):
    placed = (
        P("cfg", "req", "seq", None),
        P("cfg", "req", "seq", None),
        P("cfg", None),
        P("cfg", None, None),
        P(),
        P("req", "seq", "cfg"),
        P(None, ("req", "seq")),
        P(("req", "seq")),
        P(None, None, "req"),
        P(None, None, "req"),
        P("req", None),
        P(None, "seq"),
        P("seq", None),
        P(),
    )
    return jax.shard_map(
        on_device,
        mesh=mesh,
        in_specs=placed,
        out_specs=(P("req", "seq", "cfg"), P("req", "seq", "cfg"), P("req"), P("req")),
        check_vma=False,
    )
```

profile of v0, /device:TPU:1, one launch (start us, length us, event | category | flops | bytes accessed | tf_op | source)
XLA Modules:
  0.0 808.6 jit_solution(5461950614559532431)
XLA Ops:
  9.5 299.6 %all-gather = f32[128,120,16]{1,2,0:T(8,128)S(1)} all-gather(f32[1,120,16]{1,2,0:T(8,128)S(1)} %fusion.18), channel_id=1, replica_groups=mesh['cfg'=2,'req'=8,'seq'=16] {'req','seq'}, dimensions={0}, use_global_device_ids=true | all-gather | bytes 990720 | tf_op jit(solution)/shard_map/all_gather | solution.py:91
  314.5 19.9 %all_gather.14 = bf16[16,10,1536]{2,1,0:T(8,128)(2,1)S(1)} all-gather(bf16[2,10,1536]{2,1,0:T(8,128)(2,1)S(1)} %fusion.42), channel_id=1, replica_groups=mesh['cfg'=2,'req'=8,'seq'=16] {'req'}, dimensions={0}, use_global_device_ids=true | all-gather | bytes 552960 | tf_op jit(solution)/shard_map/all_gather | solution.py:107
  334.4 13.0 %all_to_all.30 = bf16[16,10,1536]{2,1,0:T(8,128)(2,1)S(1)} all-to-all(bf16[16,10,1536]{2,1,0:T(8,128)(2,1)S(1)} %all_gather.14), channel_id=1, replica_groups=mesh['cfg'=2,'req'=8,'seq'=16] {'seq'}, dimensions={0} | all-to-all | bytes 983040 | tf_op jit(solution)/shard_map/all_to_all | solution.py:115
  347.4 51.1 %all-gather.4.cloned.1.call-done = bf16[16,32,1536]{2,1,0:T(8,128)(2,1)} async-done(((bf16[2,32,1536]{2,1,0:T(8,128)(2,1)}), bf16[16,32,1536]{2,1,0:T(8,128)(2,1)}) %all-gather.4.cloned.1.call-update) | async-done | bytes 1572880 | tf_op jit(solution)/shard_map/all_gather | solution.py:106
  398.5 5.8 all-to-all-start
  406.0 1.7 convolution_convert_fusion.3
  407.8 13.1 %all-to-all-done = bf16[16,32,1536]{2,1,0:T(8,128)(2,1)} async-done(((bf16[16,32,1536]{2,1,0:T(8,128)(2,1)}), bf16[16,32,1536]{2,1,0:T(8,128)(2,1)}, u32[]{:S(2)}, u32[]{:S(2)}) %all-to-all-start) | async-done | bytes 1572896 | tf_op jit(solution)/shard_map/all_to_all | solution.py:114
  420.9 2.5 convolution_convert_fusion.2
  423.5 3.5 fusion.63
  427.1 2.7 fusion.17
  430.4 4.1 copy.58
  435.0 11.5 %reduce.2 = bf16[512,1536]{1,0:T(8,128)(2,1)S(1)} reduce(bf16[512,1,1536]{2,1,0:T(2,128)(2,1)} %bitcast.126, bf16[]{:T(256)} %broadcast.203), dimensions={1}, to_apply=%bitcast.124.reduce_sub_computation | reduce | bytes 3145730
  446.5 2.1 reshape.184
  448.6 18.4 %all_to_all.31 = bf16[16,2,24576]{2,1,0:T(2,128)(2,1)S(1)} all-to-all(bf16[16,2,24576]{2,1,0:T(2,128)(2,1)} %reshape.184), channel_id=1, replica_groups=mesh['cfg'=2,'req'=8,'seq'=16] {'seq'}, dimensions={0} | all-to-all | bytes 3145728 | tf_op jit(solution)/shard_map/all_to_all | solution.py:153
  466.9 6.3 reshape.185
  473.2 3.4 copy.36
  477.3 42.2 %reduce-scatter.3.cloned.1.call-done = bf16[2,32,1536]{2,1,0:T(8,128)(2,1)} async-done(((bf16[16,32,1536]{2,1,0:T(8,128)(2,1)}), bf16[2,32,1536]{2,1,0:T(8,128)(2,1)}) %reduce-scatter.3.cloned.1.call-update) | async-done | bytes 196624 | tf_op jit(solution)/shard_map/reduce_scatter | solution.py:156
  521.7 1.8 add_convert_fusion.1
  523.5 54.8 %all-gather.6.cloned.1.call-done = bf16[2,512,1536]{2,1,0:T(8,128)(2,1)} async-done(((bf16[2,32,1536]{2,1,0:T(8,128)(2,1)}), bf16[2,512,1536]{2,1,0:T(8,128)(2,1)}) %all-gather.6.cloned.1.call-update) | async-done | bytes 3145744 | tf_op jit(solution)/shard_map/all_gather | solution.py:163
  578.4 7.6 convolution_convert_fusion
  586.6 78.8 %reduce-scatter.5.cloned.1.call-done = bf16[2,32,1536]{2,1,0:T(8,128)(2,1)} async-done(((bf16[2,512,1536]{2,1,0:T(8,128)(2,1)}), bf16[2,32,1536]{2,1,0:T(8,128)(2,1)}) %reduce-scatter.5.cloned.1.call-update) | async-done | bytes 196624 | tf_op jit(solution)/shard_map/reduce_scatter | solution.py:169
  669.1 2.4 collective-permute-start
  673.1 65.3 %psum.7 = f32[2]{0:T(128)S(1)} all-reduce(f32[2]{0:T(128)S(1)} %get-tuple-element.41), channel_id=1, replica_groups=mesh['cfg'=2,'req'=8,'seq'=16] {'cfg','seq'}, use_global_device_ids=true, to_apply=%region_13.14 | all-reduce | flops 2 | bytes 16 | tf_op jit(solution)/shard_map/psum | solution.py:192
  738.8 63.2 %pmax.7 = f32[2]{0:T(128)} all-reduce(f32[2]{0:T(128)S(1)} %get-tuple-element.40), channel_id=1, replica_groups=mesh['cfg'=2,'req'=8,'seq'=16] {'cfg','seq'}, use_global_device_ids=true, to_apply=%region_15.16 | all-reduce | flops 2 | bytes 16 | tf_op jit(solution)/shard_map/pmax | solution.py:193
  (85 shorter events, 19.9 us)
Async XLA Ops:
  7.2 413.7 %copy-start = (bf16[1536,3,192]{0,2,1:T(8,128)(2,1)S(1)}, bf16[1536,3,192]{0,2,1:T(8,128)(2,1)}, u32[]{:S(2)}) copy-start(bf16[1536,3,192]{0,2,1:T(8,128)(2,1)} %param.22) | copy-start | bytes 5308420
  7.2 391.3 %all-gather.4.cloned.1.call-start = ((), (), s32[]{:S(2)}) async-start(), calls=%async_computation.5 | async-start | bytes 1769472 | tf_op jit(solution)/shard_map/all_gather | solution.py:106
  309.4 3.5 copy-start.1
  309.4 4.7 copy-start.4
  347.4 57.1 %copy-start.13 = (s32[1,16]{1,0:T(1,128)S(1)}, s32[1,16]{1,0:T(1,128)}, u32[]{:S(2)}) copy-start(s32[1,16]{1,0:T(1,128)} %param.16) | copy-start | bytes 196
  398.5 22.4 %all-to-all-start = ((bf16[16,32,1536]{2,1,0:T(8,128)(2,1)}), bf16[16,32,1536]{2,1,0:T(8,128)(2,1)}, u32[]{:S(2)}, u32[]{:S(2)}) async-start(bf16[16,32,1536]{2,1,0:T(8,128)(2,1)} %all-gather.4.cloned.1.call-done), calls=%async_computation | async-start | bytes 3145728 | tf_op jit(solution)/shard_map/all_to_all | solution.py:114
  404.3 115.1 %reduce-scatter.3.cloned.1.call-start = ((), (), s32[]{:S(2)}) async-start(), calls=%async_computation.6 | async-start | bytes 1769472 | tf_op jit(solution)/shard_map/reduce_scatter | solution.py:156
  427.1 2.7 copy-start.3
  476.5 0.7 copy-start.5
  476.5 0.7 copy-start.8
  476.5 0.7 copy-start.9
  476.5 101.8 %copy-start.11 = (bf16[384,1536]{1,0:T(8,128)(2,1)S(1)}, bf16[384,1536]{1,0:T(8,128)(2,1)}, u32[]{:S(2)}) copy-start(bf16[384,1536]{1,0:T(8,128)(2,1)} %param.26) | copy-start | bytes 3538948
  476.6 101.8 %all-gather.6.cloned.1.call-start = ((), (), s32[]{:S(2)}) async-start(), calls=%async_computation.7 | async-start | bytes 3342336 | tf_op jit(solution)/shard_map/all_gather | solution.py:163
  523.5 142.0 %reduce-scatter.5.cloned.1.call-start = ((), (), s32[]{:S(2)}) async-start(), calls=%async_computation.8 | async-start | bytes 3342336 | tf_op jit(solution)/shard_map/reduce_scatter | solution.py:169
  585.9 0.7 copy-start.6
  585.9 0.7 copy-start.7
  585.9 79.6 %copy-start.2 = (bf16[2,32,1536]{2,1,0:T(8,128)(2,1)S(1)}, bf16[2,32,1536]{2,1,0:T(8,128)(2,1)}, u32[]{:S(2)}) copy-start(bf16[2,32,1536]{2,1,0:T(8,128)(2,1)} %reduce-scatter.3.cloned.1.call-done) | copy-start | bytes 589828
  585.9 81.9 %copy-start.12 = (bf16[1536,64]{0,1:T(8,128)(2,1)S(1)}, bf16[1536,64]{0,1:T(8,128)(2,1)}, u32[]{:S(2)}) copy-start(bf16[1536,64]{0,1:T(8,128)(2,1)} %param.27) | copy-start | bytes 589828
  585.9 86.4 %copy-start.10 = (f32[2,32,32]{2,1,0:T(8,128)S(1)}, f32[2,32,32]{2,1,0:T(8,128)}, u32[]{:S(2)}) copy-start(f32[2,32,32]{2,1,0:T(8,128)} %param.19) | copy-start | bytes 24580
  669.1 3.3 collective-permute-start
Sparse Core Ops, SparseCore 0:
  314.2 84.2 all-gather.3
  476.7 42.7 reduce-scatter.2
  523.6 54.7 all-gather.5
  586.1 79.3 reduce-scatter.4
where the time goes:
time: 809 us
  blocking collectives  479 us (59%)
  waiting for transfers between devices  241 us (30%)
  other arithmetic  23.5 us (3%)
  local copies, waits for them, and re-layouts  21.2 us (3%)
  matrix products  21.1 us (3%)
  between operations  14 us (2%)
  starting transfers between devices  8.55 us (1%)
    all_gather x1, blocking collectives, on_device(): every_mod = lax.all_gather(columns, ('req', 'seq'), axis=1, tiled=True)  300 us
    reduce_scatter x1, waiting for transfers between devices, on_device(): lax.psum_scatter(mlp_terms.astype(jnp.bfloat16), 'seq', scatter_dimension...  78.8 us
    psum x1, blocking collectives, on_device(): square_total = lax.psum(squares, ('cfg', 'seq'))  65.3 us
    pmax x1, blocking collectives, on_device(): peak_value = lax.pmax(largest, ('cfg', 'seq'))  63.2 us
    all_gather x1, waiting for transfers between devices, on_device(): lax.all_gather(mlp_in, 'seq', axis=1, tiled=True)  54.8 us
    all_gather x1, waiting for transfers between devices, on_device(): lax.all_gather(img_in, 'req', axis=0, tiled=True)  51.1 us
    reduce_scatter x1, waiting for transfers between devices, on_device(): lax.psum_scatter(moved_rows.astype(jnp.bfloat16), 'req', scatter_dimensio...  42.2 us
    all_gather x1, blocking collectives, on_device(): lax.all_gather(txt_in, 'req', axis=0, tiled=True)  19.9 us
  transfers between devices with their start and end apart: 6, of which 6 were waited for; matrix products, arithmetic and copies ran while one was open for 0% of the time, Pallas kernels for 0%

commit v1 on v0

--- a/solution.py
+++ b/solution.py
@@ -13,6 +13,12 @@
 GUIDANCE = 5.0
 EPSILON = 1e-06
 MASKED_SCORE = -1e30
+
+
+def chunk_enter(block_here, dim_at):
+    v_next = list(block_here.shape[1:])
+    v_next[dim_at] *= block_here.shape[0]
+    return jnp.moveaxis(block_here, 0, dim_at).reshape(v_next)
 
 
 def from_partner(value, axis, distance):
@@ -158,11 +164,34 @@
     ).astype(jnp.float32)
     img_mid = img_float + gate_attn * attn_out
     mlp_in = (layer_norm(img_mid) * (1.0 + scale_mlp) + shift_mlp).astype(jnp.bfloat16)
+
+    def treat_words(row_data, comm_axis, at_axis=1):
+        n_parts = jax.lax.psum(1, axis_name=comm_axis)
+        sheets = [(q, (q + 1) % n_parts) for q in range(n_parts)]
+        vec_out, built = ([], [])
+        line_up = [(k, w) for w, k in sheets]
+        j = 0
+        while j < n_parts - 1:
+            if j % 2 == 0:
+                reached = jax.lax.ppermute(
+                    vec_out[-1] if vec_out else row_data, axis_name=comm_axis, perm=sheets
+                )
+                vec_out.append(reached)
+            else:
+                local_next = jax.lax.ppermute(
+                    built[-1] if built else row_data, axis_name=comm_axis, perm=line_up
+                )
+                built.append(local_next)
+            j = j + 1
+        arr_out = jnp.stack([*vec_out[::-1], row_data, *built], axis=0)
+        part_next = jax.lax.axis_index(comm_axis)
+        q_next = len(vec_out)
+        small = part_next - q_next
+        arr_out = arr_out[(jnp.arange(n_parts) - small) % n_parts]
+        return chunk_enter(arr_out, at_axis)
+
     raised = jnp.einsum(
-        "rnd,df->rnf",
-        lax.all_gather(mlp_in, "seq", axis=1, tiled=True),
-        fc_in,
-        preferred_element_type=jnp.float32,
+        "rnd,df->rnf", treat_words(mlp_in, "seq"), fc_in, preferred_element_type=jnp.float32
     )
     hidden = jax.nn.gelu(raised, approximate=True).astype(jnp.bfloat16)
     mlp_terms = jnp.einsum("rnf,fd->rnd", hidden, fc_out, preferred_element_type=jnp.float32)

time: 809 us -> 857 us (1.059)
  starting transfers between devices: 8.55 us -> 44.6 us
  local copies, waits for them, and re-layouts: 21.2 us -> 44.7 us
  waiting for transfers between devices: 241 us -> 226 us
    all_gather x1 -> x0, waiting for transfers between devices: 54.8 us -> none  [on_device(): lax.all_gather(mlp_in, 'seq', axis=1, tiled=True)]
    ppermute x0 -> x15, starting transfers between devices: none -> 35.8 us  [the longest x7 34.3 us: treat_words(): jax.lax.ppermute(built[-1] if built else row_data, axis_name=comm_axis, p...]
    ppermute x0 -> x15, waiting for transfers between devices: none -> 32.9 us  [the longest x8 32.8 us: treat_words(): jax.lax.ppermute(vec_out[-1] if vec_out else row_data, axis_name=comm_axi...]
    unnamed x39 -> x60, local copies, waits for them, and re-layouts: 15.2 us -> 29.7 us
  transfers between devices with their start and end apart: 6 -> 20, of which waited for: 6 -> 14; matrix products, arithmetic and copies ran while one was open for 0% -> 2% of each run, Pallas kernels for 0% -> 0%
where the time goes in v1:
time: 857 us; the launch traced here: 854 us
  blocking collectives  479 us (56%)
  waiting for transfers between devices  226 us (26%)
  local copies, waits for them, and re-layouts  44.7 us (5%)
  starting transfers between devices  44.6 us (5%)
  other arithmetic  23.3 us (3%)
  matrix products  21 us (2%)
  between operations  14.3 us (2%)
    all_gather x1, blocking collectives, on_device(): every_mod = lax.all_gather(columns, ('req', 'seq'), axis=1, tiled=True)  300 us
    reduce_scatter x1, waiting for transfers between devices, on_device(): lax.psum_scatter(mlp_terms.astype(jnp.bfloat16), 'seq', scatter_dimension...  86 us
    psum x1, blocking collectives, on_device(): square_total = lax.psum(squares, ('cfg', 'seq'))  65.3 us
    pmax x1, blocking collectives, on_device(): peak_value = lax.pmax(largest, ('cfg', 'seq'))  63.2 us
    all_gather x1, waiting for transfers between devices, on_device(): lax.all_gather(img_in, 'req', axis=0, tiled=True)  51 us
    reduce_scatter x1, waiting for transfers between devices, on_device(): lax.psum_scatter(moved_rows.astype(jnp.bfloat16), 'req', scatter_dimensio...  42.7 us
    ppermute x7, starting transfers between devices, treat_words(): jax.lax.ppermute(built[-1] if built else row_data, axis_name=comm_axis, p...  34.3 us
    ppermute x8, waiting for transfers between devices, treat_words(): jax.lax.ppermute(vec_out[-1] if vec_out else row_data, axis_name=comm_axi...  32.8 us
  transfers between devices with their start and end apart: 20, of which 14 were waited for; matrix products, arithmetic and copies ran while one was open for 2% of the time, Pallas kernels for 0%

profile of v1, /device:TPU:1, one launch (start us, length us, event | category | flops | bytes accessed | tf_op | source)
XLA Modules:
  0.0 853.5 jit_solution(12414763235953717062)
XLA Ops:
  10.0 299.7 %all-gather = f32[128,120,16]{1,2,0:T(8,128)S(1)} all-gather(f32[1,120,16]{1,2,0:T(8,128)S(1)} %fusion.18), channel_id=1, replica_groups=mesh['cfg'=2,'req'=8,'seq'=16] {'req','seq'}, dimensions={0}, use_global_device_ids=true | all-gather | bytes 990720 | tf_op jit(solution)/shard_map/all_gather | solution.py:97
  315.2 19.9 %all_gather.11 = bf16[16,10,1536]{2,1,0:T(8,128)(2,1)S(1)} all-gather(bf16[2,10,1536]{2,1,0:T(8,128)(2,1)S(1)} %fusion.42), channel_id=1, replica_groups=mesh['cfg'=2,'req'=8,'seq'=16] {'req'}, dimensions={0}, use_global_device_ids=true | all-gather | bytes 552960 | tf_op jit(solution)/shard_map/all_gather | solution.py:113
  335.1 13.0 %all_to_all.30 = bf16[16,10,1536]{2,1,0:T(8,128)(2,1)S(1)} all-to-all(bf16[16,10,1536]{2,1,0:T(8,128)(2,1)S(1)} %all_gather.11), channel_id=1, replica_groups=mesh['cfg'=2,'req'=8,'seq'=16] {'seq'}, dimensions={0} | all-to-all | bytes 983040 | tf_op jit(solution)/shard_map/all_to_all | solution.py:121
  348.1 51.0 %all-gather.3.cloned.1.call-done = bf16[16,32,1536]{2,1,0:T(8,128)(2,1)} async-done(((bf16[2,32,1536]{2,1,0:T(8,128)(2,1)}), bf16[16,32,1536]{2,1,0:T(8,128)(2,1)}) %all-gather.3.cloned.1.call-update) | async-done | bytes 1572880 | tf_op jit(solution)/shard_map/all_gather | solution.py:112
  399.1 5.9 all-to-all-start
  408.7 12.7 %all-to-all-done = bf16[16,32,1536]{2,1,0:T(8,128)(2,1)} async-done(((bf16[16,32,1536]{2,1,0:T(8,128)(2,1)}), bf16[16,32,1536]{2,1,0:T(8,128)(2,1)}, u32[]{:S(2)}, u32[]{:S(2)}) %all-to-all-start) | async-done | bytes 1572896 | tf_op jit(solution)/shard_map/all_to_all | solution.py:120
  435.5 11.4 %reduce.2 = bf16[512,1536]{1,0:T(8,128)(2,1)S(1)} reduce(bf16[512,1,1536]{2,1,0:T(2,128)(2,1)} %bitcast.162, bf16[]{:T(256)} %broadcast.272), dimensions={1}, to_apply=%bitcast.160.reduce_sub_computation | reduce | bytes 3145730
  449.0 18.4 %all_to_all.31 = bf16[16,2,24576]{2,1,0:T(2,128)(2,1)S(1)} all-to-all(bf16[16,2,24576]{2,1,0:T(2,128)(2,1)} %reshape.245), channel_id=1, replica_groups=mesh['cfg'=2,'req'=8,'seq'=16] {'seq'}, dimensions={0} | all-to-all | bytes 3145728 | tf_op jit(solution)/shard_map/all_to_all | solution.py:159
  467.3 6.3 reshape.246
  477.2 42.7 %reduce-scatter.3.cloned.1.call-done = bf16[2,32,1536]{2,1,0:T(8,128)(2,1)} async-done(((bf16[16,32,1536]{2,1,0:T(8,128)(2,1)}), bf16[2,32,1536]{2,1,0:T(8,128)(2,1)}) %reduce-scatter.3.cloned.1.call-update) | async-done | bytes 196624 | tf_op jit(solution)/shard_map/reduce_scatter | solution.py:162
  524.4 6.7 collective-permute-done
  531.0 4.8 collective-permute-start.8
  538.9 4.8 collective-permute-start.9
  547.1 5.1 collective-permute-start.10
  556.5 5.2 collective-permute-start.11
  561.8 4.4 collective-permute-done.4
  566.4 4.8 collective-permute-start.12
  575.4 4.8 collective-permute-start.13
  583.9 4.9 collective-permute-start.14
  607.7 4.3 gather_fusion
  616.0 7.5 convolution_convert_fusion
  624.3 86.0 %reduce-scatter.5.cloned.1.call-done = bf16[2,32,1536]{2,1,0:T(8,128)(2,1)} async-done(((bf16[2,512,1536]{2,1,0:T(8,128)(2,1)}), bf16[2,32,1536]{2,1,0:T(8,128)(2,1)}) %reduce-scatter.5.cloned.1.call-update) | async-done | bytes 196624 | tf_op jit(solution)/shard_map/reduce_scatter | solution.py:198
  717.8 65.3 %psum.7 = f32[2]{0:T(128)S(1)} all-reduce(f32[2]{0:T(128)S(1)} %get-tuple-element.41), channel_id=1, replica_groups=mesh['cfg'=2,'req'=8,'seq'=16] {'cfg','seq'}, use_global_device_ids=true, to_apply=%region_13.14 | all-reduce | flops 2 | bytes 16 | tf_op jit(solution)/shard_map/psum | solution.py:221
  783.6 63.2 %pmax.7 = f32[2]{0:T(128)} all-reduce(f32[2]{0:T(128)S(1)} %get-tuple-element.40), channel_id=1, replica_groups=mesh['cfg'=2,'req'=8,'seq'=16] {'cfg','seq'}, use_global_device_ids=true, to_apply=%region_15.16 | all-reduce | flops 2 | bytes 16 | tf_op jit(solution)/shard_map/pmax | solution.py:222
  (138 shorter events, 86.7 us)
Async XLA Ops:
  7.2 414.2 %copy-start = (bf16[1536,3,192]{0,2,1:T(8,128)(2,1)S(1)}, bf16[1536,3,192]{0,2,1:T(8,128)(2,1)}, u32[]{:S(2)}) copy-start(bf16[1536,3,192]{0,2,1:T(8,128)(2,1)} %param.22) | copy-start | bytes 5308420
  7.2 391.9 %all-gather.3.cloned.1.call-start = ((), (), s32[]{:S(2)}) async-start(), calls=%async_computation.5 | async-start | bytes 1769472 | tf_op jit(solution)/shard_map/all_gather | solution.py:112
  10.0 303.5 %copy-start.1 = (bf16[1,2,32,1536]{3,2,1,0:T(8,128)(2,1)S(1)}, bf16[1,2,32,1536]{3,2,1,0:T(8,128)(2,1)}, u32[]{:S(2)}) copy-start(bf16[1,2,32,1536]{3,2,1,0:T(8,128)(2,1)} %param.14) | copy-start | bytes 589828
  399.1 22.3 %all-to-all-start = ((bf16[16,32,1536]{2,1,0:T(8,128)(2,1)}), bf16[16,32,1536]{2,1,0:T(8,128)(2,1)}, u32[]{:S(2)}, u32[]{:S(2)}) async-start(bf16[16,32,1536]{2,1,0:T(8,128)(2,1)} %all-gather.3.cloned.1.call-done), calls=%async_computation | async-start | bytes 3145728 | tf_op jit(solution)/shard_map/all_to_all | solution.py:120
  405.0 114.8 %reduce-scatter.3.cloned.1.call-start = ((), (), s32[]{:S(2)}) async-start(), calls=%async_computation.6 | async-start | bytes 1769472 | tf_op jit(solution)/shard_map/reduce_scatter | solution.py:162
  477.1 233.2 %reduce-scatter.5.cloned.1.call-start = ((), (), s32[]{:S(2)}) async-start(), calls=%async_computation.7 | async-start | bytes 3342336 | tf_op jit(solution)/shard_map/reduce_scatter | solution.py:198
  523.1 7.9 collective-permute-start
  531.0 7.8 collective-permute-start.1
  531.0 7.8 collective-permute-start.8
  538.9 8.2 collective-permute-start.2
  538.9 8.2 collective-permute-start.9
  547.1 9.3 %collective-permute-start.3 = (bf16[2,32,1536]{2,1,0:T(8,128)(2,1)S(1)}, bf16[2,32,1536]{2,1,0:T(8,128)(2,1)S(1)}, u32[]{:S(2)}, u32[]{:S(2)}) collective-permute-start(bf16[2,32,1536]{2,1,0:T(8,128)(2,1)S(1)} %collective-permute-done.2), channel_id=1, source_target_pairs={{0,1},{1,2},{2,3},{3,4},{4,5},{5,6},{6,7},{7,8},{8,9},{9,10},{10,1... | collective-permute-start | bytes 589832 | tf_op jit(solution)/shard_map/ppermute | solution.py:176
  547.1 9.5 %collective-permute-start.10 = (bf16[2,32,1536]{2,1,0:T(8,128)(2,1)S(1)}, bf16[2,32,1536]{2,1,0:T(8,128)(2,1)S(1)}, u32[]{:S(2)}, u32[]{:S(2)}) collective-permute-start(bf16[2,32,1536]{2,1,0:T(8,128)(2,1)S(1)} %collective-permute-done.9), channel_id=1, source_target_pairs={{1,0},{2,1},{3,2},{4,3},{5,4},{6,5},{7,6},{8,7},{9,8},{10,9},{11,1... | collective-permute-start | bytes 589832 | tf_op jit(solution)/shard_map/ppermute | solution.py:181
  556.4 9.7 %collective-permute-start.4 = (bf16[2,32,1536]{2,1,0:T(8,128)(2,1)S(1)}, bf16[2,32,1536]{2,1,0:T(8,128)(2,1)S(1)}, u32[]{:S(2)}, u32[]{:S(2)}) collective-permute-start(bf16[2,32,1536]{2,1,0:T(8,128)(2,1)S(1)} %collective-permute-done.3), channel_id=1, source_target_pairs={{0,1},{1,2},{2,3},{3,4},{4,5},{5,6},{6,7},{7,8},{8,9},{9,10},{10,1... | collective-permute-start | bytes 589832 | tf_op jit(solution)/shard_map/ppermute | solution.py:176
  556.5 9.8 %collective-permute-start.11 = (bf16[2,32,1536]{2,1,0:T(8,128)(2,1)S(1)}, bf16[2,32,1536]{2,1,0:T(8,128)(2,1)S(1)}, u32[]{:S(2)}, u32[]{:S(2)}) collective-permute-start(bf16[2,32,1536]{2,1,0:T(8,128)(2,1)S(1)} %collective-permute-done.10), channel_id=1, source_target_pairs={{1,0},{2,1},{3,2},{4,3},{5,4},{6,5},{7,6},{8,7},{9,8},{10,9},{11,1... | collective-permute-start | bytes 589832 | tf_op jit(solution)/shard_map/ppermute | solution.py:181
  566.1 9.2 %collective-permute-start.5 = (bf16[2,32,1536]{2,1,0:T(8,128)(2,1)S(1)}, bf16[2,32,1536]{2,1,0:T(8,128)(2,1)}, u32[]{:S(2)}, u32[]{:S(2)}) collective-permute-start(bf16[2,32,1536]{2,1,0:T(8,128)(2,1)S(1)} %collective-permute-done.4), channel_id=1, source_target_pairs={{0,1},{1,2},{2,3},{3,4},{4,5},{5,6},{6,7},{7,8},{8,9},{9,10},{10,1... | collective-permute-start | bytes 589832 | tf_op jit(solution)/shard_map/ppermute | solution.py:176
  566.4 9.0 %collective-permute-start.12 = (bf16[2,32,1536]{2,1,0:T(8,128)(2,1)S(1)}, bf16[2,32,1536]{2,1,0:T(8,128)(2,1)}, u32[]{:S(2)}, u32[]{:S(2)}) collective-permute-start(bf16[2,32,1536]{2,1,0:T(8,128)(2,1)S(1)} %collective-permute-done.11), channel_id=1, source_target_pairs={{1,0},{2,1},{3,2},{4,3},{5,4},{6,5},{7,6},{8,7},{9,8},{10,9},{11,1... | collective-permute-start | bytes 589832 | tf_op jit(solution)/shard_map/ppermute | solution.py:181
  575.4 8.5 collective-permute-start.6
  575.4 8.5 collective-permute-start.13
  583.9 8.1 collective-permute-start.7
  583.9 23.1 %collective-permute-start.14 = (bf16[2,32,1536]{2,1,0:T(8,128)(2,1)S(1)}, bf16[2,32,1536]{2,1,0:T(8,128)(2,1)S(1)}, u32[]{:S(2)}, u32[]{:S(2)}) collective-permute-start(bf16[2,32,1536]{2,1,0:T(8,128)(2,1)S(1)} %collective-permute-done.13), channel_id=1, source_target_pairs={{1,0},{2,1},{3,2},{4,3},{5,4},{6,5},{7,6},{8,7},{9,8},{10,9},{11,1... | collective-permute-start | bytes 589832 | tf_op jit(solution)/shard_map/ppermute | solution.py:181
  623.5 92.7 %copy-start.16 = (f32[16]{0:T(128)S(1)}, f32[16]{0:T(128)}, u32[]{:S(2)}) copy-start(f32[16]{0:T(128)} %get-tuple-element.50) | copy-start | bytes 196
  623.5 93.5 %copy-start.12 = (f32[2,32,32]{2,1,0:T(8,128)S(1)}, f32[2,32,32]{2,1,0:T(8,128)}, u32[]{:S(2)}) copy-start(f32[2,32,32]{2,1,0:T(8,128)} %param.19) | copy-start | bytes 24580
  713.8 3.2 collective-permute-start.15
  (13 other events, 302.5 us)
Sparse Core Ops, SparseCore 0:
  314.9 84.1 all-gather.2
  477.2 42.6 reduce-scatter.2
  623.7 86.4 reduce-scatter.4
